TPU v7x, 512 devices: a whole 4x8x8 slice. The times are simulated.
512 devices in a mesh: dp: 16 (over z, core), mp: 32 (over x, y).
Axes of the slice: x: 4, y: 8, z: 8, core: 2. Of those that a mesh axis runs over, the one named last changes fastest.
Arguments:
- tokens: bfloat16 [2048, 4096], P(('dp', 'mp')), may hold values from -6 to 6
- hidden_grad: bfloat16 [2048, 14336], P('dp', 'mp'), may hold values from -0.125 to 0.125
- gate_weight: bfloat16 [4096, 14336], P('dp', 'mp'), may hold values from -0.09375 to 0.09375
- up_weight: bfloat16 [4096, 14336], P('dp', 'mp'), may hold values from -0.09375 to 0.09375
- gate_probe: bfloat16 [4096, 14336], P('dp', 'mp'), may hold values from -1 to 1, as said below
- gate_mean: float32 [4096, 14336], P('dp', 'mp'), may hold values from -0.6 to 0.6
- gate_curve: float32 [4096, 14336], P('dp', 'mp'), may hold values from 1 to 10
- group_counts: int32 [16], replicated, may hold values from 32 to 128, as said below
Outputs:
- gate_weight_new: bfloat16 [4096, 14336], P('dp', 'mp')
- gate_mean_new: float32 [4096, 14336], P('dp', 'mp')
- gate_curve_new: float32 [4096, 14336], P('dp', 'mp')
Inputs may be any that keep to these rules, and one draw needn't show every extreme that they name: `group_counts`: some data group has exactly 128 live tokens in every draw. `gate_probe`: every entry is -1 or 1, each sign drawn independently.
All inputs are finite; a program needn't handle non-finite values.
Results may differ from a plain program's by a relative error of at most 0.0017.
Values may be sent and summed in bfloat16 or wider, within the bound.
No kernel may reach another device: no remote copies, remote signals or barrier semaphores. Data moves between devices by JAX's collectives and lax.ppermute only.
A program may use at most 64 MiB of HBM per device.

v0:
```python
import jax
import jax.numpy as jnp
from jax import lax
from jax.sharding import PartitionSpec as P

first_decay = 0.9
second_decay = 0.999
learn_rate = 0.15
epsilon_term = 0.0001
first_fix = 1.0 - 0.9**10
second_fix = 1.0 - 0.999**10


def silu_parts(inputs):
    sigmoid_part = jax.nn.sigmoid(inputs)
    silu_slope = sigmoid_part * (1.0 + inputs * (1.0 - sigmoid_part))
    silu_bend = sigmoid_part * (1.0 - sigmoid_part) * (2.0 + inputs * (1.0 - 2.0 * sigmoid_part))
    return (silu_slope, silu_bend)


def adahessian(weight, mean_old, curve_old, gradient, probe_value, product):
    diagonal = probe_value.astype(jnp.float32) * product
    mean_new = first_decay * mean_old + (1.0 - first_decay) * gradient
    curve_new = second_decay * curve_old + (1.0 - second_decay) * diagonal * diagonal
    step_ratio = mean_new / first_fix / (jnp.sqrt(curve_new / second_fix) + epsilon_term)
    weight_new = (weight.astype(jnp.float32) - learn_rate * step_ratio).astype(jnp.bfloat16)
    return (weight_new, mean_new, curve_new)


DP = ("z", "c")
MP = ("x", "y")


def chip_ring(x, n_dp):
    n_chip = n_dp // 2
    d = lax.axis_index(DP)
    z = d // 2
    c = d % 2
    rows = x.shape[0]
    partner = [(i, i ^ 1) for i in range(n_dp)]
    ring = [(2 * j, 2 * ((j + 1) % n_chip)) for j in range(n_chip)] + [
        (2 * j + 1, 2 * ((j - 1) % n_chip) + 1) for j in range(n_chip)
    ]
    px = lax.ppermute(x, DP, partner)
    pieces = [(x, d), (px, d ^ 1)]
    cur = jnp.concatenate([x, px], 0)
    step = 2 * c - 1
    for k in range(1, n_chip // 2 + 1):
        cur = lax.ppermute(cur, DP, ring)
        j = (z + k * step) % n_chip
        o = c
        pieces.append((cur[:rows], 2 * j + o))
        pieces.append((cur[rows:], 2 * j + 1 - o))
        if k < n_chip // 2:
            ex = lax.ppermute(cur, DP, partner)
            j2 = (z - k * step) % n_chip
            o2 = 1 - c
            pieces.append((ex[:rows], 2 * j2 + o2))
            pieces.append((ex[rows:], 2 * j2 + 1 - o2))
    return pieces


def body(
    tokens, hidden_grad, gate_weight, up_weight, gate_probe, gate_mean, gate_curve, group_counts
):
    n_dp = lax.axis_size(DP)
    n_mp = lax.axis_size(MP)
    rows_loc, feat = tokens.shape
    shard = feat // n_dp
    width = gate_weight.shape[1]
    d = lax.axis_index(DP)

    def gather_mp(a):
        a = lax.all_gather(a, "y", axis=0, tiled=True)
        return lax.all_gather(a, "x", axis=0, tiled=True)

    whole = gather_mp(tokens)
    group_rows = whole.shape[0]
    t3 = tokens.reshape(rows_loc, n_dp, shard)
    a2a = lax.all_to_all(t3, DP, split_axis=1, concat_axis=1, tiled=True)
    cols = (
        gather_mp(a2a)
        .reshape(n_mp, rows_loc, n_dp, shard)
        .transpose(2, 0, 1, 3)
        .reshape(n_dp * group_rows, shard)
    )
    w3 = jnp.concatenate([gate_weight, up_weight, gate_probe], 1)
    pre = None
    for piece, s in chip_ring(w3, n_dp):
        part = lax.dynamic_slice_in_dim(whole, s * shard, shard, axis=1)
        term = jnp.dot(part, piece, preferred_element_type=jnp.float32)
        pre = term if pre is None else pre + term
    gate_pre = pre[:, :width]
    up_pre = pre[:, width : 2 * width]
    gate_tan = pre[:, 2 * width :]
    limit = lax.dynamic_index_in_dim(group_counts, d, 0, keepdims=False)
    live = (jnp.arange(group_rows, dtype=jnp.int32) < limit).astype(jnp.float32)
    silu_slope, silu_bend = silu_parts(gate_pre)
    masked = hidden_grad.astype(jnp.float32) * live[:, None]
    grad_gate = (masked * up_pre * silu_slope).astype(jnp.bfloat16)
    tan_gate = (masked * up_pre * silu_bend * gate_tan).astype(jnp.bfloat16)
    packed = jnp.concatenate([grad_gate, tan_gate], 1)
    sums = None
    for piece, g in chip_ring(packed, n_dp):
        part = lax.dynamic_slice_in_dim(cols, g * group_rows, group_rows, axis=0)
        term = lax.dot_general(
            part, piece, (((0,), (0,)), ((), ())), preferred_element_type=jnp.float32
        )
        sums = term if sums is None else sums + term
    gate_out = adahessian(
        gate_weight, gate_mean, gate_curve, sums[:, :width], gate_probe, sums[:, width:]
    )
    return (gate_out[0], gate_out[1], gate_out[2])


def solution(mesh):
    n_dp, n_mp = mesh.devices.shape
    n_x = len({dev.coords[0] for dev in mesh.devices[0]})
    mesh4 = jax.sharding.Mesh(
        mesh.devices.reshape(n_dp // 2, 2, n_x, n_mp // n_x), ("z", "c", "x", "y")
    )
    every = DP + MP
    return jax.shard_map(
        body,
        mesh=mesh4,
        in_specs=(
            P(every, None),
            P(DP, MP),
            P(DP, MP),
            P(DP, MP),
            P(DP, MP),
            P(DP, MP),
            P(DP, MP),
            P(),
        ),
        out_specs=(P(DP, MP), P(DP, MP), P(DP, MP)),
        check_vma=False,
    )
```

profile of v0, /device:TPU:4, one launch (start us, length us, event | category | flops | bytes accessed | tf_op | source)
XLA Modules:
  0.0 219.7 jit_solution(13233006125582500672)
XLA Ops:
  10.1 1.9 collective-permute-start
  12.0 2.1 collective-permute-done
  14.2 4.3 %collective-permute-start.1 = (bf16[512,1344]{0,1:T(8,128)(2,1)S(1)}, bf16[512,1344]{0,1:T(8,128)(2,1)}, u32[]{:S(2)}, u32[]{:S(2)}) collective-permute-start(bf16[512,1344]{0,1:T(8,128)(2,1)S(1)} %pad_maximum_fusion), channel_id=1, source_target_pairs={{0,64},{64,128},{128,192},{192,256},{256,320},{320,384},{384,448},... | collective-permute-start | bytes 4128776 | tf_op jit(solution)/shard_map/ppermute | solution.py:49
  18.5 26.6 %all-gather = bf16[8,4,4096]{2,1,0:T(4,128)(2,1)S(1)} all-gather(bf16[1,4,4096]{2,1,0:T(4,128)(2,1)} %bitcast.4), channel_id=1, replica_groups=mesh['z'=8,'c'=2,'x'=4,'y'=8] {'y'}, dimensions={0}, use_global_device_ids=true | all-gather | bytes 294912 | tf_op jit(solution)/shard_map/all_gather | solution.py:74
  45.9 4.4 %collective-permute-start.3 = (bf16[512,1344]{0,1:T(8,128)(2,1)}, bf16[512,1344]{0,1:T(8,128)(2,1)S(1)}, u32[]{:S(2)}, u32[]{:S(2)}) collective-permute-start(bf16[512,1344]{0,1:T(8,128)(2,1)} %collective-permute-done.1), channel_id=1, source_target_pairs={{0,64},{64,128},{128,192},{192,256},{256,320},{320,384},{384,448},... | collective-permute-start | bytes 4128776 | tf_op jit(solution)/shard_map/ppermute | solution.py:49
  50.3 8.6 %all-to-all-start = ((bf16[4,16,256]{2,0,1:T(4,128)(2,1)}), bf16[4,16,256]{2,0,1:T(4,128)(2,1)S(1)}, u32[]{:S(2)}, u32[]{:S(2)}) async-start(bf16[4,16,256]{2,0,1:T(4,128)(2,1)} %bitcast), calls=%async_computation | async-start | bytes 65536 | tf_op jit(solution)/shard_map/all_to_all | solution.py:80
  60.4 14.0 %all-to-all-done = bf16[4,16,256]{2,0,1:T(4,128)(2,1)S(1)} async-done(((bf16[4,16,256]{2,0,1:T(4,128)(2,1)}), bf16[4,16,256]{2,0,1:T(4,128)(2,1)S(1)}, u32[]{:S(2)}, u32[]{:S(2)}) %all-to-all-start) | async-done | bytes 32800 | tf_op jit(solution)/shard_map/all_to_all | solution.py:80
  74.5 26.8 %all_gather.12 = bf16[32,16,256]{2,1,0:T(8,128)(2,1)} all-gather(bf16[4,16,256]{2,1,0:T(8,128)(2,1)S(1)} %copy.28), channel_id=1, replica_groups=mesh['z'=8,'c'=2,'x'=4,'y'=8] {'y'}, dimensions={0}, use_global_device_ids=true | all-gather | bytes 294912 | tf_op jit(solution)/shard_map/all_gather | solution.py:74
  101.3 1.9 collective-permute-start.2
  104.5 1.9 collective-permute-start.5
  109.7 2.6 %collective-permute-start.4 = (bf16[512,1344]{0,1:T(8,128)(2,1)S(1)}, bf16[512,1344]{0,1:T(8,128)(2,1)S(1)}, u32[]{:S(2)}, u32[]{:S(2)}) collective-permute-start(bf16[512,1344]{0,1:T(8,128)(2,1)S(1)} %collective-permute-done.3), channel_id=1, source_target_pairs={{0,32},{32,0},{64,96},{96,64},{128,160},{160,128},{192,224},{224,1... | collective-permute-start | bytes 4128776 | tf_op jit(solution)/shard_map/ppermute | solution.py:55
  114.5 11.4 %collective-permute-done.5 = bf16[512,1344]{0,1:T(8,128)(2,1)S(1)} collective-permute-done((bf16[512,1344]{0,1:T(8,128)(2,1)S(1)}, bf16[512,1344]{0,1:T(8,128)(2,1)S(1)}, u32[]{:S(2)}, u32[]{:S(2)}) %collective-permute-start.5) | collective-permute-done | bytes 1376288 | tf_op jit(solution)/shard_map/ppermute | solution.py:49
  125.9 1.9 collective-permute-start.7
  129.3 1.9 collective-permute-start.6
  132.7 14.7 %collective-permute-done.7 = bf16[512,1344]{0,1:T(8,128)(2,1)S(1)} collective-permute-done((bf16[512,1344]{0,1:T(8,128)(2,1)S(1)}, bf16[512,1344]{0,1:T(8,128)(2,1)S(1)}, u32[]{:S(2)}, u32[]{:S(2)}) %collective-permute-start.7) | collective-permute-done | bytes 1376288 | tf_op jit(solution)/shard_map/ppermute | solution.py:49
  149.5 2.1 collective-permute-start.8
  154.9 1.9 collective-permute-start.9
  162.9 4.0 %collective-permute-done.9 = bf16[256,896]{0,1:T(8,128)(2,1)} collective-permute-done((bf16[256,896]{0,1:T(8,128)(2,1)}, bf16[256,896]{0,1:T(8,128)(2,1)}, u32[]{:S(2)}, u32[]{:S(2)}) %collective-permute-start.9) | collective-permute-done | bytes 458784 | tf_op jit(solution)/shard_map/ppermute | solution.py:49
  168.7 1.9 collective-permute-start.11
  173.2 7.3 %collective-permute-done.11 = bf16[256,896]{0,1:T(8,128)(2,1)S(1)} collective-permute-done((bf16[256,896]{0,1:T(8,128)(2,1)}, bf16[256,896]{0,1:T(8,128)(2,1)S(1)}, u32[]{:S(2)}, u32[]{:S(2)}) %collective-permute-start.11) | collective-permute-done | bytes 458784 | tf_op jit(solution)/shard_map/ppermute | solution.py:49
  182.5 1.9 collective-permute-start.13
  185.7 8.3 %collective-permute-done.13 = bf16[256,896]{0,1:T(8,128)(2,1)S(1)} collective-permute-done((bf16[256,896]{0,1:T(8,128)(2,1)S(1)}, bf16[256,896]{0,1:T(8,128)(2,1)S(1)}, u32[]{:S(2)}, u32[]{:S(2)}) %collective-permute-start.13) | collective-permute-done | bytes 458784 | tf_op jit(solution)/shard_map/ppermute | solution.py:49
  196.0 2.1 collective-permute-start.15
  199.5 8.1 %collective-permute-done.15 = bf16[256,896]{0,1:T(8,128)(2,1)S(1)} collective-permute-done((bf16[256,896]{0,1:T(8,128)(2,1)S(1)}, bf16[256,896]{0,1:T(8,128)(2,1)S(1)}, u32[]{:S(2)}, u32[]{:S(2)}) %collective-permute-start.15) | collective-permute-done | bytes 458784 | tf_op jit(solution)/shard_map/ppermute | solution.py:49
  (89 shorter events, 42.0 us)
Async XLA Ops:
  7.2 96.1 %all-gather.6.cloned.1.call-start = ((), (), s32[]{:S(2)}) async-start(), calls=%async_computation.2 | async-start | bytes 1310720 | tf_op jit(solution)/shard_map/all_gather | solution.py:75
  10.1 4.0 %collective-permute-start = (bf16[256,1344]{0,1:T(8,128)(2,1)S(1)}, bf16[256,1344]{0,1:T(8,128)(2,1)S(1)}, u32[]{:S(2)}, u32[]{:S(2)}) collective-permute-start(bf16[256,1344]{0,1:T(8,128)(2,1)S(1)} %constant_dynamic-update-slice_fusion), channel_id=1, source_target_pairs={{0,32},{32,0},{64,96},{96,64},{128,160},{160,128},{192,224},{224,1... | collective-permute-start | bytes 2064392 | tf_op jit(solution)/shard_map/ppermute | solution.py:44
  14.2 45.0 %copy-start.8 = (s32[16]{0:T(128)S(1)}, s32[16]{0:T(128)}, u32[]{:S(2)}) copy-start(s32[16]{0:T(128)} %param.15) | copy-start | bytes 196
  14.2 31.7 %collective-permute-start.1 = (bf16[512,1344]{0,1:T(8,128)(2,1)S(1)}, bf16[512,1344]{0,1:T(8,128)(2,1)}, u32[]{:S(2)}, u32[]{:S(2)}) collective-permute-start(bf16[512,1344]{0,1:T(8,128)(2,1)S(1)} %pad_maximum_fusion), channel_id=1, source_target_pairs={{0,64},{64,128},{128,192},{192,256},{256,320},{320,384},{384,448},... | collective-permute-start | bytes 4128776 | tf_op jit(solution)/shard_map/ppermute | solution.py:49
  45.9 58.6 %collective-permute-start.3 = (bf16[512,1344]{0,1:T(8,128)(2,1)}, bf16[512,1344]{0,1:T(8,128)(2,1)S(1)}, u32[]{:S(2)}, u32[]{:S(2)}) collective-permute-start(bf16[512,1344]{0,1:T(8,128)(2,1)} %collective-permute-done.1), channel_id=1, source_target_pairs={{0,64},{64,128},{128,192},{192,256},{256,320},{320,384},{384,448},... | collective-permute-start | bytes 4128776 | tf_op jit(solution)/shard_map/ppermute | solution.py:49
  50.3 24.2 %all-to-all-start = ((bf16[4,16,256]{2,0,1:T(4,128)(2,1)}), bf16[4,16,256]{2,0,1:T(4,128)(2,1)S(1)}, u32[]{:S(2)}, u32[]{:S(2)}) async-start(bf16[4,16,256]{2,0,1:T(4,128)(2,1)} %bitcast), calls=%async_computation | async-start | bytes 65536 | tf_op jit(solution)/shard_map/all_to_all | solution.py:80
  58.9 100.3 %all-gather.4.cloned.1.call-start = ((), (), s32[]{:S(2)}) async-start(), calls=%async_computation.1 | async-start | bytes 1310720 | tf_op jit(solution)/shard_map/all_gather | solution.py:75
  101.3 11.8 %collective-permute-start.2 = (bf16[512,1344]{0,1:T(8,128)(2,1)}, bf16[512,1344]{0,1:T(8,128)(2,1)}, u32[]{:S(2)}, u32[]{:S(2)}) collective-permute-start(bf16[512,1344]{0,1:T(8,128)(2,1)} %collective-permute-done.1), channel_id=1, source_target_pairs={{0,32},{32,0},{64,96},{96,64},{128,160},{160,128},{192,224},{224,1... | collective-permute-start | bytes 4128776 | tf_op jit(solution)/shard_map/ppermute | solution.py:55
  104.5 21.4 %collective-permute-start.5 = (bf16[512,1344]{0,1:T(8,128)(2,1)S(1)}, bf16[512,1344]{0,1:T(8,128)(2,1)S(1)}, u32[]{:S(2)}, u32[]{:S(2)}) collective-permute-start(bf16[512,1344]{0,1:T(8,128)(2,1)S(1)} %collective-permute-done.3), channel_id=1, source_target_pairs={{0,64},{64,128},{128,192},{192,256},{256,320},{320,384},{384,448},... | collective-permute-start | bytes 4128776 | tf_op jit(solution)/shard_map/ppermute | solution.py:49
  109.7 22.2 %collective-permute-start.4 = (bf16[512,1344]{0,1:T(8,128)(2,1)S(1)}, bf16[512,1344]{0,1:T(8,128)(2,1)S(1)}, u32[]{:S(2)}, u32[]{:S(2)}) collective-permute-start(bf16[512,1344]{0,1:T(8,128)(2,1)S(1)} %collective-permute-done.3), channel_id=1, source_target_pairs={{0,32},{32,0},{64,96},{96,64},{128,160},{160,128},{192,224},{224,1... | collective-permute-start | bytes 4128776 | tf_op jit(solution)/shard_map/ppermute | solution.py:55
  125.9 21.4 %collective-permute-start.7 = (bf16[512,1344]{0,1:T(8,128)(2,1)S(1)}, bf16[512,1344]{0,1:T(8,128)(2,1)S(1)}, u32[]{:S(2)}, u32[]{:S(2)}) collective-permute-start(bf16[512,1344]{0,1:T(8,128)(2,1)S(1)} %collective-permute-done.5), channel_id=1, source_target_pairs={{0,64},{64,128},{128,192},{192,256},{256,320},{320,384},{384,448},... | collective-permute-start | bytes 4128776 | tf_op jit(solution)/shard_map/ppermute | solution.py:49
  129.3 18.7 %collective-permute-start.6 = (bf16[512,1344]{0,1:T(8,128)(2,1)S(1)}, bf16[512,1344]{0,1:T(8,128)(2,1)S(1)}, u32[]{:S(2)}, u32[]{:S(2)}) collective-permute-start(bf16[512,1344]{0,1:T(8,128)(2,1)S(1)} %collective-permute-done.5), channel_id=1, source_target_pairs={{0,32},{32,0},{64,96},{96,64},{128,160},{160,128},{192,224},{224,1... | collective-permute-start | bytes 4128776 | tf_op jit(solution)/shard_map/ppermute | solution.py:55
  149.3 7.7 %copy-start.3 = (bf16[256,448]{0,1:T(8,128)(2,1)S(1)}, bf16[256,448]{0,1:T(8,128)(2,1)}, u32[]{:S(2)}) copy-start(bf16[256,448]{0,1:T(8,128)(2,1)} %param.10) | copy-start | bytes 688132
  149.3 8.5 %copy-start.4 = (bf16[256,448]{0,1:T(8,128)(2,1)S(1)}, bf16[256,448]{0,1:T(8,128)(2,1)}, u32[]{:S(2)}) copy-start(bf16[256,448]{0,1:T(8,128)(2,1)} %param.12) | copy-start | bytes 688132
  149.5 9.2 %copy-start.5 = (f32[256,448]{0,1:T(8,128)S(1)}, f32[256,448]{0,1:T(8,128)}, u32[]{:S(2)}) copy-start(f32[256,448]{0,1:T(8,128)} %param.13) | copy-start | bytes 1376260
  149.5 9.3 %copy-start.6 = (f32[256,448]{0,1:T(8,128)S(1)}, f32[256,448]{0,1:T(8,128)}, u32[]{:S(2)}) copy-start(f32[256,448]{0,1:T(8,128)} %param.14) | copy-start | bytes 1376260
  149.5 3.6 %collective-permute-start.8 = (bf16[128,896]{0,1:T(8,128)(2,1)S(1)}, bf16[128,896]{0,1:T(8,128)(2,1)}, u32[]{:S(2)}, u32[]{:S(2)}) collective-permute-start(bf16[128,896]{0,1:T(8,128)(2,1)S(1)} %pad_maximum_fusion.2), channel_id=1, source_target_pairs={{0,32},{32,0},{64,96},{96,64},{128,160},{160,128},{192,224},{224,1... | collective-permute-start | bytes 688136 | tf_op jit(solution)/shard_map/ppermute | solution.py:44
  154.9 11.9 %collective-permute-start.9 = (bf16[256,896]{0,1:T(8,128)(2,1)}, bf16[256,896]{0,1:T(8,128)(2,1)}, u32[]{:S(2)}, u32[]{:S(2)}) collective-permute-start(bf16[256,896]{0,1:T(8,128)(2,1)} %pad_maximum_fusion.1), channel_id=1, source_target_pairs={{0,64},{64,128},{128,192},{192,256},{256,320},{320,384},{384,448},... | collective-permute-start | bytes 1376264 | tf_op jit(solution)/shard_map/ppermute | solution.py:49
  166.8 18.2 %collective-permute-start.10 = (bf16[256,896]{0,1:T(8,128)(2,1)}, bf16[256,896]{0,1:T(8,128)(2,1)S(1)}, u32[]{:S(2)}, u32[]{:S(2)}) collective-permute-start(bf16[256,896]{0,1:T(8,128)(2,1)} %collective-permute-done.9), channel_id=1, source_target_pairs={{0,32},{32,0},{64,96},{96,64},{128,160},{160,128},{192,224},{224,1... | collective-permute-start | bytes 1376264 | tf_op jit(solution)/shard_map/ppermute | solution.py:55
  168.7 11.8 %collective-permute-start.11 = (bf16[256,896]{0,1:T(8,128)(2,1)}, bf16[256,896]{0,1:T(8,128)(2,1)S(1)}, u32[]{:S(2)}, u32[]{:S(2)}) collective-permute-start(bf16[256,896]{0,1:T(8,128)(2,1)} %collective-permute-done.9), channel_id=1, source_target_pairs={{0,64},{64,128},{128,192},{192,256},{256,320},{320,384},{384,448},... | collective-permute-start | bytes 1376264 | tf_op jit(solution)/shard_map/ppermute | solution.py:49
  180.5 18.2 %collective-permute-start.12 = (bf16[256,896]{0,1:T(8,128)(2,1)S(1)}, bf16[256,896]{0,1:T(8,128)(2,1)S(1)}, u32[]{:S(2)}, u32[]{:S(2)}) collective-permute-start(bf16[256,896]{0,1:T(8,128)(2,1)S(1)} %collective-permute-done.11), channel_id=1, source_target_pairs={{0,32},{32,0},{64,96},{96,64},{128,160},{160,128},{192,224},{224,1... | collective-permute-start | bytes 1376264 | tf_op jit(solution)/shard_map/ppermute | solution.py:55
  182.5 11.6 %collective-permute-start.13 = (bf16[256,896]{0,1:T(8,128)(2,1)S(1)}, bf16[256,896]{0,1:T(8,128)(2,1)S(1)}, u32[]{:S(2)}, u32[]{:S(2)}) collective-permute-start(bf16[256,896]{0,1:T(8,128)(2,1)S(1)} %collective-permute-done.11), channel_id=1, source_target_pairs={{0,64},{64,128},{128,192},{192,256},{256,320},{320,384},{384,448},... | collective-permute-start | bytes 1376264 | tf_op jit(solution)/shard_map/ppermute | solution.py:49
  194.0 14.1 %collective-permute-start.14 = (bf16[256,896]{0,1:T(8,128)(2,1)S(1)}, bf16[256,896]{0,1:T(8,128)(2,1)S(1)}, u32[]{:S(2)}, u32[]{:S(2)}) collective-permute-start(bf16[256,896]{0,1:T(8,128)(2,1)S(1)} %collective-permute-done.13), channel_id=1, source_target_pairs={{0,32},{32,0},{64,96},{96,64},{128,160},{160,128},{192,224},{224,1... | collective-permute-start | bytes 1376264 | tf_op jit(solution)/shard_map/ppermute | solution.py:55
  196.0 11.6 %collective-permute-start.15 = (bf16[256,896]{0,1:T(8,128)(2,1)S(1)}, bf16[256,896]{0,1:T(8,128)(2,1)S(1)}, u32[]{:S(2)}, u32[]{:S(2)}) collective-permute-start(bf16[256,896]{0,1:T(8,128)(2,1)S(1)} %collective-permute-done.13), channel_id=1, source_target_pairs={{0,64},{64,128},{128,192},{192,256},{256,320},{320,384},{384,448},... | collective-permute-start | bytes 1376264 | tf_op jit(solution)/shard_map/ppermute | solution.py:49
  (4 other events, 6.1 us)
Sparse Core Ops, SparseCore 0:
  46.0 30.7 all-gather.5
  101.4 24.4 all-gather.3
where the time goes:
time: 221 us; the launch traced here: 220 us
  waiting for transfers between devices  71.6 us (32%)
  blocking collectives  53.4 us (24%)
  starting transfers between devices  45.2 us (20%)
  matrix products  19 us (9%)
  between operations  15 us (7%)
  local copies, waits for them, and re-layouts  12.3 us (6%)
  other arithmetic  3.25 us (1%)
    ppermute x8, waiting for transfers between devices, chip_ring(): cur = lax.ppermute(cur, DP, ring)  53.8 us
    all_gather x2, blocking collectives, gather_mp(): a = lax.all_gather(a, 'y', axis=0, tiled=True)  53.4 us
    ppermute x8, starting transfers between devices, chip_ring(): cur = lax.ppermute(cur, DP, ring)  20.3 us
    all_to_all x1, waiting for transfers between devices, body(): a2a = lax.all_to_all(t3, DP, split_axis=1, concat_axis=1, tiled=True)  14 us
    ppermute x6, starting transfers between devices, chip_ring(): ex = lax.ppermute(cur, DP, partner)  12.2 us
    dot_general x16, matrix products, body(): term = jnp.dot(part, piece, preferred_element_type=jnp.float32)  10.9 us
    unnamed x28, local copies, waits for them, and re-layouts  8.65 us
    all_to_all x1, starting transfers between devices, body(): a2a = lax.all_to_all(t3, DP, split_axis=1, concat_axis=1, tiled=True)  8.58 us
  transfers between devices with their start and end apart: 19, of which 9 were waited for; matrix products, arithmetic and copies ran while one was open for 12% of the time, Pallas kernels for 0%

commit v1 on v0

--- a/solution.py
+++ b/solution.py
@@ -71,7 +71,7 @@
     d = lax.axis_index(DP)
 
     def gather_mp(a):
-        a = lax.all_gather(a, "y", axis=0, tiled=True)
+        a = jnp.concatenate(lax.all_to_all(jnp.stack([a] * lax.axis_size("y")), "y", 0, 0), axis=0)
         return lax.all_gather(a, "x", axis=0, tiled=True)
 
     whole = gather_mp(tokens)

time: 221 us -> 204 us (0.923)
  the two profiles are of different devices: /device:TPU:4 before, /device:TPU:2 now
where the time goes in v1:
time: 204 us; the launch traced here: 203 us
  waiting for transfers between devices  71.7 us (35%)
  starting transfers between devices  40.3 us (20%)
  blocking collectives  39.8 us (20%)
  matrix products  19 us (9%)
  between operations  15 us (7%)
  local copies, waits for them, and re-layouts  13.9 us (7%)
  other arithmetic  3.25 us (2%)
    ppermute x8, waiting for transfers between devices, chip_ring(): cur = lax.ppermute(cur, DP, ring)  57.5 us
    all_to_all x1, blocking collectives, body(): a2a = lax.all_to_all(t3, DP, split_axis=1, concat_axis=1, tiled=True)  22.4 us
    ppermute x8, starting transfers between devices, chip_ring(): cur = lax.ppermute(cur, DP, ring)  19.6 us
    all_to_all x1, blocking collectives, gather_mp(): lax.all_to_all(jnp.stack([a] * lax.axis_size('y')), 'y', 0, 0)  17.4 us
    ppermute x6, starting transfers between devices, chip_ring(): ex = lax.ppermute(cur, DP, partner)  11.5 us
    dot_general x16, matrix products, body(): term = jnp.dot(part, piece, preferred_element_type=jnp.float32)  10.9 us
    all_to_all x1, waiting for transfers between devices, gather_mp(): lax.all_to_all(jnp.stack([a] * lax.axis_size('y')), 'y', 0, 0)  10.4 us
    dot_general x16, matrix products, body(): lax.dot_general(part, piece, (((0,), (0,)), ((), ())), preferred_element_...  8.18 us
  transfers between devices with their start and end apart: 19, of which 10 were waited for; matrix products, arithmetic and copies ran while one was open for 14% of the time, Pallas kernels for 0%

profile of v1, /device:TPU:2, one launch (start us, length us, event | category | flops | bytes accessed | tf_op | source)
XLA Modules:
  0.0 203.0 jit_solution(2128038573988500716)
XLA Ops:
  10.1 1.9 collective-permute-start
  12.0 2.1 %collective-permute-done = bf16[256,1344]{0,1:T(8,128)(2,1)S(1)} collective-permute-done((bf16[256,1344]{0,1:T(8,128)(2,1)S(1)}, bf16[256,1344]{0,1:T(8,128)(2,1)S(1)}, u32[]{:S(2)}, u32[]{:S(2)}) %collective-permute-start) | collective-permute-done | bytes 688160 | tf_op jit(solution)/shard_map/ppermute | solution.py:44
  14.2 4.3 %collective-permute-start.1 = (bf16[512,1344]{0,1:T(8,128)(2,1)S(1)}, bf16[512,1344]{0,1:T(8,128)(2,1)}, u32[]{:S(2)}, u32[]{:S(2)}) collective-permute-start(bf16[512,1344]{0,1:T(8,128)(2,1)S(1)} %pad_maximum_fusion), channel_id=1, source_target_pairs={{0,64},{64,128},{128,192},{192,256},{256,320},{320,384},{384,448},... | collective-permute-start | bytes 4128776 | tf_op jit(solution)/shard_map/ppermute | solution.py:49
  18.6 17.4 %all_to_all.15 = bf16[8,4,4096]{2,1,0:T(4,128)(2,1)S(1)} all-to-all(bf16[8,4,4096]{2,1,0:T(4,128)(2,1)S(1)} %stack.5), channel_id=1, replica_groups=mesh['z'=8,'c'=2,'x'=4,'y'=8] {'y'}, dimensions={0} | all-to-all | bytes 524288 | tf_op jit(solution)/shard_map/all_to_all | solution.py:74
  36.8 4.8 %collective-permute-done.1 = bf16[512,1344]{0,1:T(8,128)(2,1)} collective-permute-done((bf16[512,1344]{0,1:T(8,128)(2,1)S(1)}, bf16[512,1344]{0,1:T(8,128)(2,1)}, u32[]{:S(2)}, u32[]{:S(2)}) %collective-permute-start.1) | collective-permute-done | bytes 1376288 | tf_op jit(solution)/shard_map/ppermute | solution.py:49
  43.5 22.4 %all_to_all.16 = bf16[4,16,256]{2,0,1:T(4,128)(2,1)S(1)} all-to-all(bf16[4,16,256]{2,0,1:T(4,128)(2,1)S(1)} %bitcast.13), channel_id=1, replica_groups=mesh['z'=8,'c'=2,'x'=4,'y'=8] {'z','c'}, dimensions={1} | all-to-all | bytes 65536 | tf_op jit(solution)/shard_map/all_to_all | solution.py:80
  66.7 5.2 %all-to-all-start.1 = ((bf16[8,4,16,256]{3,1,2,0:T(4,128)(2,1)}), bf16[8,4,16,256]{3,1,2,0:T(4,128)(2,1)S(1)}, u32[]{:S(2)}, u32[]{:S(2)}) async-start(bf16[8,4,16,256]{3,1,2,0:T(4,128)(2,1)} %stack.4), calls=%async_computation.1 | async-start | bytes 524288 | tf_op jit(solution)/shard_map/all_to_all | solution.py:74
  73.4 10.4 %all-to-all-done.1 = bf16[8,4,16,256]{3,1,2,0:T(4,128)(2,1)S(1)} async-done(((bf16[8,4,16,256]{3,1,2,0:T(4,128)(2,1)}), bf16[8,4,16,256]{3,1,2,0:T(4,128)(2,1)S(1)}, u32[]{:S(2)}, u32[]{:S(2)}) %all-to-all-start.1) | async-done | bytes 262176 | tf_op jit(solution)/shard_map/all_to_all | solution.py:74
  84.6 1.9 collective-permute-start.2
  87.9 3.4 %collective-permute-start.5 = (bf16[512,1344]{0,1:T(8,128)(2,1)S(1)}, bf16[512,1344]{0,1:T(8,128)(2,1)S(1)}, u32[]{:S(2)}, u32[]{:S(2)}) collective-permute-start(bf16[512,1344]{0,1:T(8,128)(2,1)S(1)} %collective-permute-done.3), channel_id=1, source_target_pairs={{0,64},{64,128},{128,192},{192,256},{256,320},{320,384},{384,448},... | collective-permute-start | bytes 4128776 | tf_op jit(solution)/shard_map/ppermute | solution.py:49
  94.6 1.9 collective-permute-start.4
  98.7 10.6 %collective-permute-done.5 = bf16[512,1344]{0,1:T(8,128)(2,1)S(1)} collective-permute-done((bf16[512,1344]{0,1:T(8,128)(2,1)S(1)}, bf16[512,1344]{0,1:T(8,128)(2,1)S(1)}, u32[]{:S(2)}, u32[]{:S(2)}) %collective-permute-start.5) | collective-permute-done | bytes 1376288 | tf_op jit(solution)/shard_map/ppermute | solution.py:49
  109.3 2.2 %collective-permute-start.7 = (bf16[512,1344]{0,1:T(8,128)(2,1)S(1)}, bf16[512,1344]{0,1:T(8,128)(2,1)S(1)}, u32[]{:S(2)}, u32[]{:S(2)}) collective-permute-start(bf16[512,1344]{0,1:T(8,128)(2,1)S(1)} %collective-permute-done.5), channel_id=1, source_target_pairs={{0,64},{64,128},{128,192},{192,256},{256,320},{320,384},{384,448},... | collective-permute-start | bytes 4128776 | tf_op jit(solution)/shard_map/ppermute | solution.py:49
  112.9 1.9 collective-permute-start.6
  116.3 14.4 %collective-permute-done.7 = bf16[512,1344]{0,1:T(8,128)(2,1)S(1)} collective-permute-done((bf16[512,1344]{0,1:T(8,128)(2,1)S(1)}, bf16[512,1344]{0,1:T(8,128)(2,1)S(1)}, u32[]{:S(2)}, u32[]{:S(2)}) %collective-permute-start.7) | collective-permute-done | bytes 1376288 | tf_op jit(solution)/shard_map/ppermute | solution.py:49
  132.9 2.1 %collective-permute-start.8 = (bf16[128,896]{0,1:T(8,128)(2,1)S(1)}, bf16[128,896]{0,1:T(8,128)(2,1)}, u32[]{:S(2)}, u32[]{:S(2)}) collective-permute-start(bf16[128,896]{0,1:T(8,128)(2,1)S(1)} %pad_maximum_fusion.2), channel_id=1, source_target_pairs={{0,32},{32,0},{64,96},{96,64},{128,160},{160,128},{192,224},{224,1... | collective-permute-start | bytes 688136 | tf_op jit(solution)/shard_map/ppermute | solution.py:44
  138.3 1.9 collective-permute-start.9
  146.2 4.0 %collective-permute-done.9 = bf16[256,896]{0,1:T(8,128)(2,1)} collective-permute-done((bf16[256,896]{0,1:T(8,128)(2,1)}, bf16[256,896]{0,1:T(8,128)(2,1)}, u32[]{:S(2)}, u32[]{:S(2)}) %collective-permute-start.9) | collective-permute-done | bytes 458784 | tf_op jit(solution)/shard_map/ppermute | solution.py:49
  152.1 1.9 collective-permute-start.11
  156.5 7.3 %collective-permute-done.11 = bf16[256,896]{0,1:T(8,128)(2,1)S(1)} collective-permute-done((bf16[256,896]{0,1:T(8,128)(2,1)}, bf16[256,896]{0,1:T(8,128)(2,1)S(1)}, u32[]{:S(2)}, u32[]{:S(2)}) %collective-permute-start.11) | collective-permute-done | bytes 458784 | tf_op jit(solution)/shard_map/ppermute | solution.py:49
  165.8 1.9 collective-permute-start.13
  169.1 8.3 %collective-permute-done.13 = bf16[256,896]{0,1:T(8,128)(2,1)S(1)} collective-permute-done((bf16[256,896]{0,1:T(8,128)(2,1)S(1)}, bf16[256,896]{0,1:T(8,128)(2,1)S(1)}, u32[]{:S(2)}, u32[]{:S(2)}) %collective-permute-start.13) | collective-permute-done | bytes 458784 | tf_op jit(solution)/shard_map/ppermute | solution.py:49
  179.3 2.1 %collective-permute-start.15 = (bf16[256,896]{0,1:T(8,128)(2,1)S(1)}, bf16[256,896]{0,1:T(8,128)(2,1)S(1)}, u32[]{:S(2)}, u32[]{:S(2)}) collective-permute-start(bf16[256,896]{0,1:T(8,128)(2,1)S(1)} %collective-permute-done.13), channel_id=1, source_target_pairs={{0,64},{64,128},{128,192},{192,256},{256,320},{320,384},{384,448},... | collective-permute-start | bytes 1376264 | tf_op jit(solution)/shard_map/ppermute | solution.py:49
  182.8 8.1 %collective-permute-done.15 = bf16[256,896]{0,1:T(8,128)(2,1)S(1)} collective-permute-done((bf16[256,896]{0,1:T(8,128)(2,1)S(1)}, bf16[256,896]{0,1:T(8,128)(2,1)S(1)}, u32[]{:S(2)}, u32[]{:S(2)}) %collective-permute-start.15) | collective-permute-done | bytes 458784 | tf_op jit(solution)/shard_map/ppermute | solution.py:49
  (93 shorter events, 45.5 us)
Async XLA Ops:
  7.2 79.4 %all-gather.5.cloned.1.call-start = ((), (), s32[]{:S(2)}) async-start(), calls=%async_computation.4 | async-start | bytes 1310720 | tf_op jit(solution)/shard_map/all_gather | solution.py:75
  10.1 8.5 %copy-start.7 = (bf16[4,4096]{1,0:T(4,128)(2,1)S(1)}, bf16[4,4096]{1,0:T(4,128)(2,1)}, u32[]{:S(2)}) copy-start(bf16[4,4096]{1,0:T(4,128)(2,1)} %param.8) | copy-start | bytes 98308
  10.1 4.0 %collective-permute-start = (bf16[256,1344]{0,1:T(8,128)(2,1)S(1)}, bf16[256,1344]{0,1:T(8,128)(2,1)S(1)}, u32[]{:S(2)}, u32[]{:S(2)}) collective-permute-start(bf16[256,1344]{0,1:T(8,128)(2,1)S(1)} %constant_dynamic-update-slice_fusion), channel_id=1, source_target_pairs={{0,32},{32,0},{64,96},{96,64},{128,160},{160,128},{192,224},{224,1... | collective-permute-start | bytes 2064392 | tf_op jit(solution)/shard_map/ppermute | solution.py:44
  14.2 27.3 %collective-permute-start.1 = (bf16[512,1344]{0,1:T(8,128)(2,1)S(1)}, bf16[512,1344]{0,1:T(8,128)(2,1)}, u32[]{:S(2)}, u32[]{:S(2)}) collective-permute-start(bf16[512,1344]{0,1:T(8,128)(2,1)S(1)} %pad_maximum_fusion), channel_id=1, source_target_pairs={{0,64},{64,128},{128,192},{192,256},{256,320},{320,384},{384,448},... | collective-permute-start | bytes 4128776 | tf_op jit(solution)/shard_map/ppermute | solution.py:49
  18.6 53.6 %copy-start.9 = (s32[16]{0:T(128)S(1)}, s32[16]{0:T(128)}, u32[]{:S(2)}) copy-start(s32[16]{0:T(128)} %param.15) | copy-start | bytes 196
  41.6 46.3 %collective-permute-start.3 = (bf16[512,1344]{0,1:T(8,128)(2,1)}, bf16[512,1344]{0,1:T(8,128)(2,1)S(1)}, u32[]{:S(2)}, u32[]{:S(2)}) collective-permute-start(bf16[512,1344]{0,1:T(8,128)(2,1)} %collective-permute-done.1), channel_id=1, source_target_pairs={{0,64},{64,128},{128,192},{192,256},{256,320},{320,384},{384,448},... | collective-permute-start | bytes 4128776 | tf_op jit(solution)/shard_map/ppermute | solution.py:49
  66.7 17.2 %all-to-all-start.1 = ((bf16[8,4,16,256]{3,1,2,0:T(4,128)(2,1)}), bf16[8,4,16,256]{3,1,2,0:T(4,128)(2,1)S(1)}, u32[]{:S(2)}, u32[]{:S(2)}) async-start(bf16[8,4,16,256]{3,1,2,0:T(4,128)(2,1)} %stack.4), calls=%async_computation.1 | async-start | bytes 524288 | tf_op jit(solution)/shard_map/all_to_all | solution.py:74
  71.9 70.7 %all-gather.3.cloned.1.call-start = ((), (), s32[]{:S(2)}) async-start(), calls=%async_computation.3 | async-start | bytes 1310720 | tf_op jit(solution)/shard_map/all_gather | solution.py:75
  84.6 12.6 %collective-permute-start.2 = (bf16[512,1344]{0,1:T(8,128)(2,1)}, bf16[512,1344]{0,1:T(8,128)(2,1)}, u32[]{:S(2)}, u32[]{:S(2)}) collective-permute-start(bf16[512,1344]{0,1:T(8,128)(2,1)} %collective-permute-done.1), channel_id=1, source_target_pairs={{0,32},{32,0},{64,96},{96,64},{128,160},{160,128},{192,224},{224,1... | collective-permute-start | bytes 4128776 | tf_op jit(solution)/shard_map/ppermute | solution.py:55
  87.9 21.4 %collective-permute-start.5 = (bf16[512,1344]{0,1:T(8,128)(2,1)S(1)}, bf16[512,1344]{0,1:T(8,128)(2,1)S(1)}, u32[]{:S(2)}, u32[]{:S(2)}) collective-permute-start(bf16[512,1344]{0,1:T(8,128)(2,1)S(1)} %collective-permute-done.3), channel_id=1, source_target_pairs={{0,64},{64,128},{128,192},{192,256},{256,320},{320,384},{384,448},... | collective-permute-start | bytes 4128776 | tf_op jit(solution)/shard_map/ppermute | solution.py:49
  94.6 21.0 %collective-permute-start.4 = (bf16[512,1344]{0,1:T(8,128)(2,1)S(1)}, bf16[512,1344]{0,1:T(8,128)(2,1)S(1)}, u32[]{:S(2)}, u32[]{:S(2)}) collective-permute-start(bf16[512,1344]{0,1:T(8,128)(2,1)S(1)} %collective-permute-done.3), channel_id=1, source_target_pairs={{0,32},{32,0},{64,96},{96,64},{128,160},{160,128},{192,224},{224,1... | collective-permute-start | bytes 4128776 | tf_op jit(solution)/shard_map/ppermute | solution.py:55
  109.3 21.4 %collective-permute-start.7 = (bf16[512,1344]{0,1:T(8,128)(2,1)S(1)}, bf16[512,1344]{0,1:T(8,128)(2,1)S(1)}, u32[]{:S(2)}, u32[]{:S(2)}) collective-permute-start(bf16[512,1344]{0,1:T(8,128)(2,1)S(1)} %collective-permute-done.5), channel_id=1, source_target_pairs={{0,64},{64,128},{128,192},{192,256},{256,320},{320,384},{384,448},... | collective-permute-start | bytes 4128776 | tf_op jit(solution)/shard_map/ppermute | solution.py:49
  112.9 18.5 %collective-permute-start.6 = (bf16[512,1344]{0,1:T(8,128)(2,1)S(1)}, bf16[512,1344]{0,1:T(8,128)(2,1)S(1)}, u32[]{:S(2)}, u32[]{:S(2)}) collective-permute-start(bf16[512,1344]{0,1:T(8,128)(2,1)S(1)} %collective-permute-done.5), channel_id=1, source_target_pairs={{0,32},{32,0},{64,96},{96,64},{128,160},{160,128},{192,224},{224,1... | collective-permute-start | bytes 4128776 | tf_op jit(solution)/shard_map/ppermute | solution.py:55
  132.6 8.5 %copy-start.4 = (bf16[256,448]{0,1:T(8,128)(2,1)S(1)}, bf16[256,448]{0,1:T(8,128)(2,1)}, u32[]{:S(2)}) copy-start(bf16[256,448]{0,1:T(8,128)(2,1)} %param.12) | copy-start | bytes 688132
  132.8 9.2 %copy-start.5 = (f32[256,448]{0,1:T(8,128)S(1)}, f32[256,448]{0,1:T(8,128)}, u32[]{:S(2)}) copy-start(f32[256,448]{0,1:T(8,128)} %param.13) | copy-start | bytes 1376260
  132.9 9.3 %copy-start.6 = (f32[256,448]{0,1:T(8,128)S(1)}, f32[256,448]{0,1:T(8,128)}, u32[]{:S(2)}) copy-start(f32[256,448]{0,1:T(8,128)} %param.14) | copy-start | bytes 1376260
  132.9 3.6 %collective-permute-start.8 = (bf16[128,896]{0,1:T(8,128)(2,1)S(1)}, bf16[128,896]{0,1:T(8,128)(2,1)}, u32[]{:S(2)}, u32[]{:S(2)}) collective-permute-start(bf16[128,896]{0,1:T(8,128)(2,1)S(1)} %pad_maximum_fusion.2), channel_id=1, source_target_pairs={{0,32},{32,0},{64,96},{96,64},{128,160},{160,128},{192,224},{224,1... | collective-permute-start | bytes 688136 | tf_op jit(solution)/shard_map/ppermute | solution.py:44
  138.3 11.9 %collective-permute-start.9 = (bf16[256,896]{0,1:T(8,128)(2,1)}, bf16[256,896]{0,1:T(8,128)(2,1)}, u32[]{:S(2)}, u32[]{:S(2)}) collective-permute-start(bf16[256,896]{0,1:T(8,128)(2,1)} %pad_maximum_fusion.1), channel_id=1, source_target_pairs={{0,64},{64,128},{128,192},{192,256},{256,320},{320,384},{384,448},... | collective-permute-start | bytes 1376264 | tf_op jit(solution)/shard_map/ppermute | solution.py:49
  150.2 18.2 %collective-permute-start.10 = (bf16[256,896]{0,1:T(8,128)(2,1)}, bf16[256,896]{0,1:T(8,128)(2,1)S(1)}, u32[]{:S(2)}, u32[]{:S(2)}) collective-permute-start(bf16[256,896]{0,1:T(8,128)(2,1)} %collective-permute-done.9), channel_id=1, source_target_pairs={{0,32},{32,0},{64,96},{96,64},{128,160},{160,128},{192,224},{224,1... | collective-permute-start | bytes 1376264 | tf_op jit(solution)/shard_map/ppermute | solution.py:55
  152.1 11.8 %collective-permute-start.11 = (bf16[256,896]{0,1:T(8,128)(2,1)}, bf16[256,896]{0,1:T(8,128)(2,1)S(1)}, u32[]{:S(2)}, u32[]{:S(2)}) collective-permute-start(bf16[256,896]{0,1:T(8,128)(2,1)} %collective-permute-done.9), channel_id=1, source_target_pairs={{0,64},{64,128},{128,192},{192,256},{256,320},{320,384},{384,448},... | collective-permute-start | bytes 1376264 | tf_op jit(solution)/shard_map/ppermute | solution.py:49
  163.9 18.2 %collective-permute-start.12 = (bf16[256,896]{0,1:T(8,128)(2,1)S(1)}, bf16[256,896]{0,1:T(8,128)(2,1)S(1)}, u32[]{:S(2)}, u32[]{:S(2)}) collective-permute-start(bf16[256,896]{0,1:T(8,128)(2,1)S(1)} %collective-permute-done.11), channel_id=1, source_target_pairs={{0,32},{32,0},{64,96},{96,64},{128,160},{160,128},{192,224},{224,1... | collective-permute-start | bytes 1376264 | tf_op jit(solution)/shard_map/ppermute | solution.py:55
  165.8 11.6 %collective-permute-start.13 = (bf16[256,896]{0,1:T(8,128)(2,1)S(1)}, bf16[256,896]{0,1:T(8,128)(2,1)S(1)}, u32[]{:S(2)}, u32[]{:S(2)}) collective-permute-start(bf16[256,896]{0,1:T(8,128)(2,1)S(1)} %collective-permute-done.11), channel_id=1, source_target_pairs={{0,64},{64,128},{128,192},{192,256},{256,320},{320,384},{384,448},... | collective-permute-start | bytes 1376264 | tf_op jit(solution)/shard_map/ppermute | solution.py:49
  177.4 14.1 %collective-permute-start.14 = (bf16[256,896]{0,1:T(8,128)(2,1)S(1)}, bf16[256,896]{0,1:T(8,128)(2,1)S(1)}, u32[]{:S(2)}, u32[]{:S(2)}) collective-permute-start(bf16[256,896]{0,1:T(8,128)(2,1)S(1)} %collective-permute-done.13), channel_id=1, source_target_pairs={{0,32},{32,0},{64,96},{96,64},{128,160},{160,128},{192,224},{224,1... | collective-permute-start | bytes 1376264 | tf_op jit(solution)/shard_map/ppermute | solution.py:55
  179.3 11.6 %collective-permute-start.15 = (bf16[256,896]{0,1:T(8,128)(2,1)S(1)}, bf16[256,896]{0,1:T(8,128)(2,1)S(1)}, u32[]{:S(2)}, u32[]{:S(2)}) collective-permute-start(bf16[256,896]{0,1:T(8,128)(2,1)S(1)} %collective-permute-done.13), channel_id=1, source_target_pairs={{0,64},{64,128},{128,192},{192,256},{256,320},{320,384},{384,448},... | collective-permute-start | bytes 1376264 | tf_op jit(solution)/shard_map/ppermute | solution.py:49
  (5 other events, 15.2 us)
Sparse Core Ops, SparseCore 0:
  37.0 26.8 all-gather.4
  84.7 21.4 all-gather.2
